TPU v7x, 32 devices: a whole 2x2x4 slice. The times are simulated.
32 devices in a mesh: group: 2 (over y), ctx: 4 (over z), head: 2 (over x), sub: 2 (over core).
Axes of the slice: x: 2, y: 2, z: 4, core: 2. Of those that a mesh axis runs over, the one named last changes fastest.
Arguments:
- queries: bfloat16 [4, 4096, 128], P(('head', 'sub'), ('group', 'ctx')), parts along dimension 1, may hold values from -18 to 18
- keys: bfloat16 [4, 4096, 128], P(('head', 'sub'), ('group', 'ctx')), parts along dimension 1, may hold values from -6 to 6
- values: bfloat16 [4, 4096, 128], P(('head', 'sub'), ('group', 'ctx')), parts along dimension 1, may hold values from -6 to 6
- stick_offset: float32 [4], P(('head', 'sub')), may hold values from -14 to -7
Outputs:
- attended: bfloat16 [4, 4096, 128], P(('head', 'sub'), ('group', 'ctx')), parts along dimension 1
There are 2 independent parts, one for each index of `group`. A program takes and returns all parts, laid end to end along the dimension named above; an argument that names none is the same for every part. Nothing has to cross between parts.
All inputs are finite; a program needn't handle non-finite values.
Results may differ from a plain program's by a relative error of at most 0.0049.
Values may be sent and summed in bfloat16 or wider, within the bound.
No kernel may reach another device: no remote copies, remote signals or barrier semaphores. Data moves between devices by JAX's collectives and lax.ppermute only.
A program may use at most 64 MiB of HBM per device.

v0:
```python
import functools
import math

import jax
import numpy as np
import jax.numpy as jnp
from jax import lax
from jax.experimental import pallas as pl
from jax.experimental.pallas import tpu as pltpu
from jax.sharding import PartitionSpec as P


ROW_TILE = 256
LOG2E = 1.4426950408889634
LN2 = 0.6931471805599453


def pair_kernel(scalar_ref, q_ref, kv_ref, upper_ref, *refs, mode, scale):
    diag = mode == "diag"
    if mode == "step":
        in_summed_ref, in_spent_ref, summed_ref, spent_ref = refs
    else:
        summed_ref = refs[0]
    tile, _ = q_ref.shape
    keys = kv_ref.shape[0] // 2
    score = (
        lax.dot_general(
            q_ref[...],
            kv_ref[:keys, :],
            (((1,), (1,)), ((), ())),
            preferred_element_type=jnp.float32,
        )
        * (scale * LOG2E)
        + scalar_ref[0] * LOG2E
    )
    spent = jnp.maximum(score, 0.0) + jnp.log2(1.0 + jnp.exp2(-jnp.abs(score)))
    if diag:
        row = pl.program_id(0) * tile + lax.broadcasted_iota(jnp.int32, (tile, keys), 0)
        col = lax.broadcasted_iota(jnp.int32, (tile, keys), 1)
        live = col < row
        spent = jnp.where(live, spent, 0.0)
    upper = upper_ref[...]
    high = spent.astype(jnp.bfloat16)
    low = (spent - high.astype(jnp.float32)).astype(jnp.bfloat16)
    later = jnp.dot(high, upper, preferred_element_type=jnp.float32) + jnp.dot(
        low, upper, preferred_element_type=jnp.float32
    )
    weight = jnp.exp2((score - spent) - later)
    if diag:
        weight = jnp.where(live, weight, 0.0)
    part = jnp.dot(weight.astype(jnp.bfloat16), kv_ref[keys:, :], preferred_element_type=jnp.float32)
    if mode == "far":
        summed_ref[...] = part.astype(summed_ref.dtype)
        return
    tot = (later[:, 0:1] + spent[:, 0:1]) * LN2
    if diag:
        summed_ref[...] = part
        refs[1][...] = tot
        return
    use = scalar_ref[1] > 0.0
    before = in_spent_ref[...]
    summed_ref[...] = jnp.where(use, in_summed_ref[...] + jnp.exp(-before) * part, in_summed_ref[...])
    spent_ref[...] = jnp.where(use, before + tot, before)


def pair_terms(q, kv, upper, scalars, carried=None, mode="step"):
    rows, width = q.shape
    keys = kv.shape[0] // 2
    tile = min(ROW_TILE, rows)
    kernel = functools.partial(pair_kernel, mode=mode, scale=1.0 / math.sqrt(width))
    flops = 2 * rows * keys * (2 * width + 2 * keys)
    rows_spec = pl.BlockSpec((tile, width), lambda r: (r, 0))
    col_spec = pl.BlockSpec((tile, 1), lambda r: (r, 0))
    in_specs = [
        pl.BlockSpec(memory_space=pltpu.SMEM),
        rows_spec,
        pl.BlockSpec(memory_space=pltpu.VMEM),
        pl.BlockSpec((keys, keys), lambda r: (0, 0)),
    ]
    args = [scalars, q, kv, upper]
    if mode == "step":
        in_specs += [rows_spec, col_spec]
        args += list(carried)
    out_specs = [rows_spec]
    out_shape = [jax.ShapeDtypeStruct((rows, width), jnp.bfloat16 if mode == "far" else jnp.float32)]
    if mode != "far":
        out_specs.append(col_spec)
        out_shape.append(jax.ShapeDtypeStruct((rows, 1), jnp.float32))
    return pl.pallas_call(
        kernel,
        grid=(rows // tile,),
        in_specs=in_specs,
        out_specs=out_specs,
        out_shape=out_shape,
        cost_estimate=pl.CostEstimate(
            flops=flops, transcendentals=3 * rows * keys, bytes_accessed=rows * width * 16
        ),
    )(*args)


def one_head(q_own, k_own, v_own, offset):
    count = lax.axis_size("ctx")
    place = lax.axis_index("ctx")
    up = [(i, i + 1) for i in range(count - 1)]
    down = [(i, i - 1) for i in range(1, count)]
    keys = k_own.shape[0]
    upper = jnp.asarray(np.triu(np.ones((keys, keys), np.float32), 1).T, jnp.bfloat16)
    kv = jnp.concatenate([k_own, v_own], axis=0)
    steps = jnp.arange(count, dtype=jnp.int32)
    table = jnp.stack(
        [jnp.broadcast_to(offset, (count,)), jnp.where(place >= steps, 1.0, 0.0)], axis=1
    ).astype(jnp.float32)
    summed, spent = pair_terms(q_own, kv, upper, table[0], mode="diag")
    if count == 1:
        return summed.astype(jnp.bfloat16)
    for step in range(1, count - 1):
        kv = lax.ppermute(kv, "ctx", up)
        if step == 1:
            q_next = lax.ppermute(q_own, "ctx", down)
        if step < count - 2:
            summed, spent = pair_terms(q_own, kv, upper, table[step], (summed, spent))
    if count == 2:
        q_next = lax.ppermute(q_own, "ctx", down)
    far = pair_terms(q_next, kv, upper, table[0], mode="far")[0]
    far = lax.ppermute(far, "ctx", up)
    if count > 2:
        summed, spent = pair_terms(
            q_own, kv, upper, table[count - 2], (summed, spent)
        )
    out = jnp.where(
        place == count - 1, summed + jnp.exp(-spent) * far.astype(jnp.float32), summed
    )
    return out.astype(jnp.bfloat16)


def on_device(queries, keys, values, stick_offset):
    results = []
    for h in range(queries.shape[0]):
        results.append(one_head(queries[h], keys[h], values[h], stick_offset[h]))
    return jnp.stack(results, axis=0)


def solution(mesh):
    placed = (
        P(("head", "sub"), ("group", "ctx"), None),
        P(("head", "sub"), ("group", "ctx"), None),
        P(("head", "sub"), ("group", "ctx"), None),
        P(("head", "sub")),
    )
    return jax.shard_map(
        on_device,
        mesh=mesh,
        in_specs=placed,
        out_specs=P(("head", "sub"), ("group", "ctx"), None),
        check_vma=False,
    )
```

profile of v0, /device:TPU:0, one launch (start us, length us, event | category | flops | bytes accessed | tf_op | source)
XLA Modules:
  0.0 38.7 jit_solution(18398671241768790269)
XLA Ops:
  0.0 0.0 copy-start.4
  0.0 1.0 %pad_maximum_fusion.kv_ref = bf16[1024,128]{1,0:T(8,128)(2,1)S(1)} fusion(bf16[512,128]{1,0:T(8,128)(2,1)} %bitcast.13, bf16[512,128]{1,0:T(8,128)(2,1)} %bitcast.14), kind=kLoop, calls=%fused_computation.2 | loop fusion | flops 524288 | bytes 524288 | tf_op jit(solution)/shard_map/concatenate | solution.py:108
  1.0 0.0 copy-start.1
  1.0 5.0 %collective-permute-start = (bf16[1024,128]{1,0:T(8,128)(2,1)S(1)}, bf16[1024,128]{1,0:T(8,128)(2,1)S(1)}, u32[]{:S(2)}, u32[]{:S(2)}) collective-permute-start(bf16[1024,128]{1,0:T(8,128)(2,1)S(1)} %pad_maximum_fusion.kv_ref), channel_id=1, source_target_pairs={{0,4},{4,8},{8,12},{1,5},{5,9},{9,13},{2,6},{6,10},{10,14},{3,7},{... | collective-permute-start | bytes 786440 | tf_op jit(solution)/shard_map/ppermute | solution.py:117
  6.0 0.0 copy-done.4
  6.0 1.3 %collective-permute-start.2 = (bf16[512,128]{1,0:T(8,128)(2,1)S(1)}, bf16[512,128]{1,0:T(8,128)(2,1)S(1)}, u32[]{:S(2)}, u32[]{:S(2)}) collective-permute-start(bf16[512,128]{1,0:T(8,128)(2,1)S(1)} %bitcast.18), channel_id=1, source_target_pairs={{4,0},{8,4},{12,8},{5,1},{9,5},{13,9},{6,2},{10,6},{14,10},{7,3},{... | collective-permute-start | bytes 393224 | tf_op jit(solution)/shard_map/ppermute | solution.py:119
  7.3 4.2 %collective-permute-done.kv_ref = bf16[1024,128]{1,0:T(8,128)(2,1)S(1)} collective-permute-done((bf16[1024,128]{1,0:T(8,128)(2,1)S(1)}, bf16[1024,128]{1,0:T(8,128)(2,1)S(1)}, u32[]{:S(2)}, u32[]{:S(2)}) %collective-permute-start) | collective-permute-done | bytes 262176 | tf_op jit(solution)/shard_map/ppermute | solution.py:117
  11.5 0.0 copy-start.2
  11.6 4.4 %collective-permute-start.1 = (bf16[1024,128]{1,0:T(8,128)(2,1)S(1)}, bf16[1024,128]{1,0:T(8,128)(2,1)S(1)}, u32[]{:S(2)}, u32[]{:S(2)}) collective-permute-start(bf16[1024,128]{1,0:T(8,128)(2,1)S(1)} %collective-permute-done.kv_ref), channel_id=1, source_target_pairs={{0,4},{4,8},{8,12},{1,5},{5,9},{9,13},{2,6},{6,10},{10,14},{3,7},{... | collective-permute-start | bytes 786440 | tf_op jit(solution)/shard_map/ppermute | solution.py:117
  16.6 0.7 %fusion.5 = (f32[2]{0:T(128)}, f32[2]{0:T(128)}, f32[2]{0:T(128)}) fusion(f32[4,1]{1,0:T(4,128)S(1)} %fusion.2, f32[]{:T(128)} %bitcast.12), kind=kLoop, calls=%fused_computation.12 | loop fusion | bytes 44 | tf_op jit(solution)/shard_map/squeeze | solution.py:113
  17.3 0.0 copy-done.1
  17.3 3.6 %shard_map.55 = (f32[512,128]{1,0:T(8,128)}, f32[512,1]{1,0:T(8,128)}) custom-call(f32[2]{0:T(128)} %get-tuple-element.17.scalar_ref, bf16[512,128]{1,0:T(8,128)(2,1)} %bitcast.15, bf16[1024,128]{1,0:T(8,128)(2,1)} %copy-done.1, bf16[512,512]{1,0:T(8,128)(2,1)} %constant.13.clone.upper_ref), custom_call_target="tpu_custom_call" | custom-call | flops 671088640 | bytes 1048576 | tf_op jit(solution)/shard_map/pallas_call | solution.py:89
  20.9 0.0 copy-done.2
  20.9 3.8 %shard_map.56 = (f32[512,128]{1,0:T(8,128)}, f32[512,1]{1,0:T(8,128)}) custom-call(f32[2]{0:T(128)} %get-tuple-element.18.scalar_ref, bf16[512,128]{1,0:T(8,128)(2,1)} %bitcast.16, bf16[1024,128]{1,0:T(8,128)(2,1)} %copy-done.2, bf16[512,512]{1,0:T(8,128)(2,1)} %constant.13.clone.upper_ref, f32[512,128]{1,0:T(8,128)} %get-tuple-element.11.refs_0_, ...), custom_call_target="tpu_custom_call" | custom-call | flops 671088640 | bytes 1048576 | tf_op jit(solution)/shard_map/pallas_call | solution.py:89
  24.7 0.0 collective-permute-done.2.q_ref
  24.7 0.0 copy-start.5
  24.7 0.0 collective-permute-done.1.kv_ref
  24.7 0.6 %copy-done.5 = bf16[512,128]{1,0:T(8,128)(2,1)} copy-done((bf16[512,128]{1,0:T(8,128)(2,1)}, bf16[512,128]{1,0:T(8,128)(2,1)S(1)}, u32[]{:S(2)}) %copy-start.5) | copy-done | bytes 131096
  25.3 0.0 copy-start.3
  25.3 0.7 %copy-done.3 = bf16[1024,128]{1,0:T(8,128)(2,1)} copy-done((bf16[1024,128]{1,0:T(8,128)(2,1)}, bf16[1024,128]{1,0:T(8,128)(2,1)S(1)}, u32[]{:S(2)}) %copy-start.3) | copy-done | bytes 262168
  26.0 3.5 %shard_map.58 = bf16[512,128]{1,0:T(8,128)(2,1)} custom-call(f32[2]{0:T(128)} %get-tuple-element.17.scalar_ref, bf16[512,128]{1,0:T(8,128)(2,1)} %copy-done.5, bf16[1024,128]{1,0:T(8,128)(2,1)} %copy-done.3, bf16[512,512]{1,0:T(8,128)(2,1)} %constant.13.clone.upper_ref), custom_call_target="tpu_custom_call" | custom-call | flops 671088640 | bytes 1048576 | tf_op jit(solution)/shard_map/pallas_call | solution.py:89
  29.5 3.5 %collective-permute-start.3 = (bf16[512,128]{1,0:T(8,128)(2,1)}, bf16[512,128]{1,0:T(8,128)(2,1)S(1)}, u32[]{:S(2)}, u32[]{:S(2)}) collective-permute-start(bf16[512,128]{1,0:T(8,128)(2,1)} %shard_map.58), channel_id=1, source_target_pairs={{0,4},{4,8},{8,12},{1,5},{5,9},{9,13},{2,6},{6,10},{10,14},{3,7},{... | collective-permute-start | bytes 393224 | tf_op jit(solution)/shard_map/ppermute | solution.py:125
  33.0 3.8 %shard_map.57 = (f32[512,128]{1,0:T(8,128)}, f32[512,1]{1,0:T(8,128)}) custom-call(f32[2]{0:T(128)} %get-tuple-element.19.scalar_ref, bf16[512,128]{1,0:T(8,128)(2,1)} %bitcast.17, bf16[1024,128]{1,0:T(8,128)(2,1)} %copy-done.3, bf16[512,512]{1,0:T(8,128)(2,1)} %constant.13.clone.upper_ref, f32[512,128]{1,0:T(8,128)} %get-tuple-element.13.refs_0_, ...), custom_call_target="tpu_custom_call" | custom-call | flops 671088640 | bytes 1048576 | tf_op jit(solution)/shard_map/pallas_call | solution.py:89
  36.7 0.0 copy-start
  36.7 1.1 %exponential_reduce_fusion = f32[512]{0:T(512)S(1)} fusion(f32[512,1]{1,0:T(8,128)} %get-tuple-element.16), kind=kLoop, calls=%fused_computation.3 | loop fusion | flops 512 | bytes 4096 | tf_op jit(solution)/shard_map/exp | solution.py:131
  37.9 0.0 collective-permute-done.3
  37.9 0.0 copy-done
  37.9 0.8 %fusion.1 = bf16[1,512,128]{2,1,0:T(8,128)(2,1)} fusion(f32[512,128]{1,0:T(8,128)S(1)} %copy-done, bf16[512,128]{1,0:T(8,128)(2,1)S(1)} %collective-permute-done.3, f32[512]{0:T(512)S(1)} %exponential_reduce_fusion, pred[]{:T(512)S(6)} %eq.3), kind=kLoop, calls=%fused_computation.4 | loop fusion | flops 327680 | bytes 526337 | tf_op jit(solution)/shard_map/stack | solution.py:140
  (1 shorter events, 0.0 us)
Async XLA Ops:
  0.0 6.0 %copy-start.4 = (bf16[1,512,128]{2,1,0:T(8,128)(2,1)S(1)}, bf16[1,512,128]{2,1,0:T(8,128)(2,1)}, u32[]{:S(2)}) copy-start(bf16[1,512,128]{2,1,0:T(8,128)(2,1)} %param.5) | copy-start | bytes 393220
  1.0 16.3 %copy-start.1 = (bf16[1024,128]{1,0:T(8,128)(2,1)}, bf16[1024,128]{1,0:T(8,128)(2,1)S(1)}, u32[]{:S(2)}) copy-start(bf16[1024,128]{1,0:T(8,128)(2,1)S(1)} %pad_maximum_fusion.kv_ref) | copy-start | bytes 786436
  1.0 10.5 %collective-permute-start = (bf16[1024,128]{1,0:T(8,128)(2,1)S(1)}, bf16[1024,128]{1,0:T(8,128)(2,1)S(1)}, u32[]{:S(2)}, u32[]{:S(2)}) collective-permute-start(bf16[1024,128]{1,0:T(8,128)(2,1)S(1)} %pad_maximum_fusion.kv_ref), channel_id=1, source_target_pairs={{0,4},{4,8},{8,12},{1,5},{5,9},{9,13},{2,6},{6,10},{10,14},{3,7},{... | collective-permute-start | bytes 786440 | tf_op jit(solution)/shard_map/ppermute | solution.py:117
  6.0 18.6 %collective-permute-start.2 = (bf16[512,128]{1,0:T(8,128)(2,1)S(1)}, bf16[512,128]{1,0:T(8,128)(2,1)S(1)}, u32[]{:S(2)}, u32[]{:S(2)}) collective-permute-start(bf16[512,128]{1,0:T(8,128)(2,1)S(1)} %bitcast.18), channel_id=1, source_target_pairs={{4,0},{8,4},{12,8},{5,1},{9,5},{13,9},{6,2},{10,6},{14,10},{7,3},{... | collective-permute-start | bytes 393224 | tf_op jit(solution)/shard_map/ppermute | solution.py:119
  11.5 9.3 %copy-start.2 = (bf16[1024,128]{1,0:T(8,128)(2,1)}, bf16[1024,128]{1,0:T(8,128)(2,1)S(1)}, u32[]{:S(2)}) copy-start(bf16[1024,128]{1,0:T(8,128)(2,1)S(1)} %collective-permute-done.kv_ref) | copy-start | bytes 786436
  11.6 13.1 %collective-permute-start.1 = (bf16[1024,128]{1,0:T(8,128)(2,1)S(1)}, bf16[1024,128]{1,0:T(8,128)(2,1)S(1)}, u32[]{:S(2)}, u32[]{:S(2)}) collective-permute-start(bf16[1024,128]{1,0:T(8,128)(2,1)S(1)} %collective-permute-done.kv_ref), channel_id=1, source_target_pairs={{0,4},{4,8},{8,12},{1,5},{5,9},{9,13},{2,6},{6,10},{10,14},{3,7},{... | collective-permute-start | bytes 786440 | tf_op jit(solution)/shard_map/ppermute | solution.py:117
  24.7 0.7 %copy-start.5 = (bf16[512,128]{1,0:T(8,128)(2,1)}, bf16[512,128]{1,0:T(8,128)(2,1)S(1)}, u32[]{:S(2)}) copy-start(bf16[512,128]{1,0:T(8,128)(2,1)S(1)} %collective-permute-done.2.q_ref) | copy-start | bytes 393220
  25.3 0.7 %copy-start.3 = (bf16[1024,128]{1,0:T(8,128)(2,1)}, bf16[1024,128]{1,0:T(8,128)(2,1)S(1)}, u32[]{:S(2)}) copy-start(bf16[1024,128]{1,0:T(8,128)(2,1)S(1)} %collective-permute-done.1.kv_ref) | copy-start | bytes 786436
  29.5 8.4 %collective-permute-start.3 = (bf16[512,128]{1,0:T(8,128)(2,1)}, bf16[512,128]{1,0:T(8,128)(2,1)S(1)}, u32[]{:S(2)}, u32[]{:S(2)}) collective-permute-start(bf16[512,128]{1,0:T(8,128)(2,1)} %shard_map.58), channel_id=1, source_target_pairs={{0,4},{4,8},{8,12},{1,5},{5,9},{9,13},{2,6},{6,10},{10,14},{3,7},{... | collective-permute-start | bytes 393224 | tf_op jit(solution)/shard_map/ppermute | solution.py:125
  36.7 1.2 %copy-start = (f32[512,128]{1,0:T(8,128)S(1)}, f32[512,128]{1,0:T(8,128)}, u32[]{:S(2)}) copy-start(f32[512,128]{1,0:T(8,128)} %get-tuple-element.15) | copy-start | bytes 786436
where the time goes:
time: 39 us; the launch traced here: 38.7 us
  Pallas kernels  14.6 us (37%)
  starting transfers between devices  14.1 us (36%)
  waiting for transfers between devices  4.22 us (11%)
  other arithmetic  2.97 us (8%)
  local copies, waits for them, and re-layouts  2.03 us (5%)
  between operations  0.76 us (2%)
    pallas_call x4, Pallas kernels, pair_terms(): pl.pallas_call(kernel, grid=(rows // tile,), in_specs=in_specs, out_specs...  14.6 us
    ppermute x2, starting transfers between devices, one_head(): kv = lax.ppermute(kv, 'ctx', up)  9.36 us
    ppermute x2, waiting for transfers between devices, one_head(): kv = lax.ppermute(kv, 'ctx', up)  4.22 us
    ppermute x1, starting transfers between devices, one_head(): far = lax.ppermute(far, 'ctx', up)  3.46 us
    unnamed x12, local copies, waits for them, and re-layouts  1.35 us
    ppermute x1, starting transfers between devices, one_head(): q_next = lax.ppermute(q_own, 'ctx', down)  1.29 us
    exp x1, other arithmetic, one_head(): jnp.exp(-spent) * far.astype(jnp.float32)  1.14 us
    concatenate x1, other arithmetic, one_head(): kv = jnp.concatenate([k_own, v_own], axis=0)  1.02 us
  transfers between devices with their start and end apart: 4, of which 1 were waited for; matrix products, arithmetic and copies ran while one was open for 5% of the time, Pallas kernels for 29%

commit v1 on v0

--- a/solution.py
+++ b/solution.py
@@ -101,35 +101,35 @@
 def one_head(q_own, k_own, v_own, offset):
     count = lax.axis_size("ctx")
     place = lax.axis_index("ctx")
-    up = [(i, i + 1) for i in range(count - 1)]
-    down = [(i, i - 1) for i in range(1, count)]
+    up = [(i, (i + 1) % count) for i in range(count)]
+    down = [(i, (i - 1) % count) for i in range(count)]
+    rows = q_own.shape[0]
     keys = k_own.shape[0]
     upper = jnp.asarray(np.triu(np.ones((keys, keys), np.float32), 1).T, jnp.bfloat16)
-    kv = jnp.concatenate([k_own, v_own], axis=0)
+    own_kv = jnp.concatenate([k_own, v_own], axis=0)
     steps = jnp.arange(count, dtype=jnp.int32)
     table = jnp.stack(
         [jnp.broadcast_to(offset, (count,)), jnp.where(place >= steps, 1.0, 0.0)], axis=1
     ).astype(jnp.float32)
-    summed, spent = pair_terms(q_own, kv, upper, table[0], mode="diag")
+    summed, spent = pair_terms(q_own, own_kv, upper, table[0], mode="diag")
     if count == 1:
         return summed.astype(jnp.bfloat16)
+    if count == 2:
+        kv = lax.ppermute(own_kv, "ctx", up)
+        summed, spent = pair_terms(q_own, kv, upper, table[1], (summed, spent))
+        return summed.astype(jnp.bfloat16)
+    last = place == count - 1
+    sent = jnp.concatenate([jnp.where(last, q_own, k_own), v_own], axis=0)
+    kv = lax.ppermute(sent, "ctx", up)
+    far = pair_terms(kv[:rows], own_kv, upper, table[0], mode="far")[0]
     for step in range(1, count - 1):
-        kv = lax.ppermute(kv, "ctx", up)
-        if step == 1:
-            q_next = lax.ppermute(q_own, "ctx", down)
+        if step > 1:
+            kv = lax.ppermute(kv, "ctx", up)
         if step < count - 2:
             summed, spent = pair_terms(q_own, kv, upper, table[step], (summed, spent))
-    if count == 2:
-        q_next = lax.ppermute(q_own, "ctx", down)
-    far = pair_terms(q_next, kv, upper, table[0], mode="far")[0]
-    far = lax.ppermute(far, "ctx", up)
-    if count > 2:
-        summed, spent = pair_terms(
-            q_own, kv, upper, table[count - 2], (summed, spent)
-        )
-    out = jnp.where(
-        place == count - 1, summed + jnp.exp(-spent) * far.astype(jnp.float32), summed
-    )
+    far = lax.ppermute(far, "ctx", down)
+    summed, spent = pair_terms(q_own, kv, upper, table[count - 2], (summed, spent))
+    out = jnp.where(last, summed + jnp.exp(-spent) * far.astype(jnp.float32), summed)
     return out.astype(jnp.bfloat16)
 
 

time: 39 us -> 35.8 us (0.918)
  starting transfers between devices: 14.1 us -> 6.87 us
  waiting for transfers between devices: 4.22 us -> 7.67 us
  other arithmetic: 2.97 us -> 3.71 us
    ppermute x2 -> x1, starting transfers between devices: 9.36 us -> 0.01 us  [one_head(): kv = lax.ppermute(kv, 'ctx', up)]
    ppermute x2, waiting for transfers between devices: 0.01 us -> 7.66 us  [the longest x1 7.66 us: one_head(): kv = lax.ppermute(sent, 'ctx', up)]
    ppermute x2 -> x1, waiting for transfers between devices: 4.22 us -> 0.01 us  [one_head(): kv = lax.ppermute(kv, 'ctx', up)]
    ppermute x2, starting transfers between devices: 4.75 us -> 6.87 us  [the longest x1 3.82 us: one_head(): far = lax.ppermute(far, 'ctx', down)]
    select_n x0 -> x1, other arithmetic: none -> 1.03 us  [one_head(): sent = jnp.concatenate([jnp.where(last, q_own, k_own), v_own], axis=0)]
    slice x0 -> x1, local copies, waits for them, and re-layouts: none -> 0.66 us  [one_head(): far = pair_terms(kv[:rows], own_kv, upper, table[0], mode='far')[0]]
    unnamed x12 -> x10, local copies, waits for them, and re-layouts: 1.35 us -> 0.75 us
  transfers between devices with their start and end apart: 4 -> 3, of which waited for: 1 -> 1; matrix products, arithmetic and copies ran while one was open for 5% -> 7% of each run, Pallas kernels for 29% -> 41%
where the time goes in v1:
time: 35.8 us; the launch traced here: 35.6 us
  Pallas kernels  14.6 us (41%)
  waiting for transfers between devices  7.67 us (21%)
  starting transfers between devices  6.87 us (19%)
  other arithmetic  3.71 us (10%)
  local copies, waits for them, and re-layouts  2.07 us (6%)
  between operations  0.71 us (2%)
    pallas_call x4, Pallas kernels, pair_terms(): pl.pallas_call(kernel, grid=(rows // tile,), in_specs=in_specs, out_specs...  14.6 us
    ppermute x1, waiting for transfers between devices, one_head(): kv = lax.ppermute(sent, 'ctx', up)  7.66 us
    ppermute x1, starting transfers between devices, one_head(): far = lax.ppermute(far, 'ctx', down)  3.82 us
    ppermute x1, starting transfers between devices, one_head(): kv = lax.ppermute(sent, 'ctx', up)  3.05 us
    exp x1, other arithmetic, one_head(): jnp.exp(-spent) * far.astype(jnp.float32)  1.14 us
    select_n x1, other arithmetic, one_head(): sent = jnp.concatenate([jnp.where(last, q_own, k_own), v_own], axis=0)  1.03 us
    another operation x1, other arithmetic, on_device(): return jnp.stack(results, axis=0)  0.8 us
    unnamed x10, local copies, waits for them, and re-layouts  0.75 us
  transfers between devices with their start and end apart: 3, of which 1 were waited for; matrix products, arithmetic and copies ran while one was open for 7% of the time, Pallas kernels for 41%

profile of v1, /device:TPU:0, one launch (start us, length us, event | category | flops | bytes accessed | tf_op | source)
XLA Modules:
  0.0 35.6 jit_solution(14788280742783100341)
XLA Ops:
  0.0 0.0 copy-start
  0.0 0.0 copy-start.2
  0.0 1.0 %broadcast_select_fusion = bf16[512,128]{1,0:T(8,128)(2,1)S(1)} fusion(pred[]{:T(512)S(6)} %eq.3, bf16[1,512,128]{2,1,0:T(8,128)(2,1)} %param.6, bf16[1,512,128]{2,1,0:T(8,128)(2,1)} %param.5), kind=kLoop, calls=%fused_computation.6 | loop fusion | flops 65536 | bytes 393217 | tf_op jit(solution)/shard_map/jit(_where)/select_n | solution.py:122
  1.0 0.0 copy-done
  1.0 0.0 copy-done.2
  1.1 0.7 %pad_maximum_fusion = (bf16[1024,128]{1,0:T(8,128)(2,1)}, bf16[1024,128]{1,0:T(8,128)(2,1)S(1)}) fusion(bf16[512,128]{1,0:T(8,128)(2,1)S(1)} %bitcast.16, bf16[512,128]{1,0:T(8,128)(2,1)S(1)} %bitcast.15, bf16[512,128]{1,0:T(8,128)(2,1)S(1)} %broadcast_select_fusion), kind=kLoop, calls=%fused_computation.1 | loop fusion | flops 917504 | bytes 917504 | tf_op jit(solution)/shard_map/concatenate | solution.py:109
  1.8 3.1 %collective-permute-start = (bf16[1024,128]{1,0:T(8,128)(2,1)S(1)}, bf16[1024,128]{1,0:T(8,128)(2,1)S(1)}, u32[]{:S(2)}, u32[]{:S(2)}) collective-permute-start(bf16[1024,128]{1,0:T(8,128)(2,1)S(1)} %get-tuple-element.18), channel_id=1, source_target_pairs={{0,4},{4,8},{8,12},{12,0},{1,5},{5,9},{9,13},{13,1},{2,6},{6,10},{... | collective-permute-start | bytes 786440 | tf_op jit(solution)/shard_map/ppermute | solution.py:123
  5.6 7.7 %collective-permute-done.kv_ref = bf16[1024,128]{1,0:T(8,128)(2,1)S(1)} collective-permute-done((bf16[1024,128]{1,0:T(8,128)(2,1)S(1)}, bf16[1024,128]{1,0:T(8,128)(2,1)S(1)}, u32[]{:S(2)}, u32[]{:S(2)}) %collective-permute-start) | collective-permute-done | bytes 262176 | tf_op jit(solution)/shard_map/ppermute | solution.py:123
  13.2 0.0 copy-start.3
  13.2 0.0 collective-permute-start.1
  13.2 0.7 %fusion.5 = (f32[2]{0:T(128)}, f32[2]{0:T(128)}, f32[2]{0:T(128)}) fusion(f32[4,1]{1,0:T(4,128)S(1)} %fusion.2, f32[]{:T(128)} %bitcast.14), kind=kLoop, calls=%fused_computation.14 | loop fusion | bytes 44 | tf_op jit(solution)/shard_map/squeeze | solution.py:114
  13.9 3.6 %shard_map.55 = (f32[512,128]{1,0:T(8,128)}, f32[512,1]{1,0:T(8,128)}) custom-call(f32[2]{0:T(128)} %get-tuple-element.19.scalar_ref, bf16[512,128]{1,0:T(8,128)(2,1)} %bitcast.17, bf16[1024,128]{1,0:T(8,128)(2,1)} %get-tuple-element.17.kv_ref, bf16[512,512]{1,0:T(8,128)(2,1)} %constant.13.clone.upper_ref), custom_call_target="tpu_custom_call" | custom-call | flops 671088640 | bytes 1048576 | tf_op jit(solution)/shard_map/pallas_call | solution.py:89
  17.5 0.0 copy-done.3
  17.5 0.7 %slice.17.q_ref = bf16[512,128]{1,0:T(8,128)(2,1)} slice(bf16[1024,128]{1,0:T(8,128)(2,1)S(1)} %collective-permute-done.kv_ref), slice={[0:512], [0:128]} | slice | bytes 262144 | tf_op jit(solution)/shard_map/slice | solution.py:124
  18.1 3.5 %shard_map.58 = bf16[512,128]{1,0:T(8,128)(2,1)} custom-call(f32[2]{0:T(128)} %get-tuple-element.19.scalar_ref, bf16[512,128]{1,0:T(8,128)(2,1)} %slice.17.q_ref, bf16[1024,128]{1,0:T(8,128)(2,1)} %get-tuple-element.17.kv_ref, bf16[512,512]{1,0:T(8,128)(2,1)} %constant.13.clone.upper_ref), custom_call_target="tpu_custom_call" | custom-call | flops 671088640 | bytes 1048576 | tf_op jit(solution)/shard_map/pallas_call | solution.py:89
  21.6 3.8 %collective-permute-start.2 = (bf16[512,128]{1,0:T(8,128)(2,1)}, bf16[512,128]{1,0:T(8,128)(2,1)S(1)}, u32[]{:S(2)}, u32[]{:S(2)}) collective-permute-start(bf16[512,128]{1,0:T(8,128)(2,1)} %shard_map.58), channel_id=1, source_target_pairs={{0,12},{4,0},{8,4},{12,8},{1,13},{5,1},{9,5},{13,9},{2,14},{6,2},{... | collective-permute-start | bytes 393224 | tf_op jit(solution)/shard_map/ppermute | solution.py:130
  25.4 3.7 %shard_map.56 = (f32[512,128]{1,0:T(8,128)}, f32[512,1]{1,0:T(8,128)}) custom-call(f32[2]{0:T(128)} %get-tuple-element.20.scalar_ref, bf16[512,128]{1,0:T(8,128)(2,1)} %bitcast.18, bf16[1024,128]{1,0:T(8,128)(2,1)} %copy-done.3, bf16[512,512]{1,0:T(8,128)(2,1)} %constant.13.clone.upper_ref, f32[512,128]{1,0:T(8,128)} %get-tuple-element.11.refs_0_, ...), custom_call_target="tpu_custom_call" | custom-call | flops 671088640 | bytes 1048576 | tf_op jit(solution)/shard_map/pallas_call | solution.py:89
  29.2 0.0 collective-permute-done.1.kv_ref
  29.2 0.0 copy-start.4
  29.2 0.7 %copy-done.4 = bf16[1024,128]{1,0:T(8,128)(2,1)} copy-done((bf16[1024,128]{1,0:T(8,128)(2,1)}, bf16[1024,128]{1,0:T(8,128)(2,1)S(1)}, u32[]{:S(2)}) %copy-start.4) | copy-done | bytes 262168
  29.9 3.8 %shard_map.57 = (f32[512,128]{1,0:T(8,128)}, f32[512,1]{1,0:T(8,128)}) custom-call(f32[2]{0:T(128)} %get-tuple-element.21.scalar_ref, bf16[512,128]{1,0:T(8,128)(2,1)} %bitcast.19, bf16[1024,128]{1,0:T(8,128)(2,1)} %copy-done.4, bf16[512,512]{1,0:T(8,128)(2,1)} %constant.13.clone.upper_ref, f32[512,128]{1,0:T(8,128)} %get-tuple-element.13.refs_0_, ...), custom_call_target="tpu_custom_call" | custom-call | flops 671088640 | bytes 1048576 | tf_op jit(solution)/shard_map/pallas_call | solution.py:89
  33.6 0.0 copy-start.1
  33.6 1.1 %exponential_reduce_fusion = f32[512]{0:T(512)S(1)} fusion(f32[512,1]{1,0:T(8,128)} %get-tuple-element.16), kind=kLoop, calls=%fused_computation.4 | loop fusion | flops 512 | bytes 4096 | tf_op jit(solution)/shard_map/exp | solution.py:132
  34.8 0.0 collective-permute-done.2
  34.8 0.0 copy-done.1
  34.8 0.8 %fusion.1 = bf16[1,512,128]{2,1,0:T(8,128)(2,1)} fusion(f32[512,128]{1,0:T(8,128)S(1)} %copy-done.1, bf16[512,128]{1,0:T(8,128)(2,1)S(1)} %collective-permute-done.2, f32[512]{0:T(512)S(1)} %exponential_reduce_fusion, pred[]{:T(512)S(6)} %eq.3), kind=kLoop, calls=%fused_computation.5 | loop fusion | flops 327680 | bytes 526337 | tf_op jit(solution)/shard_map/stack | solution.py:140
  (1 shorter events, 0.0 us)
Async XLA Ops:
  0.0 1.0 %copy-start = (bf16[1,512,128]{2,1,0:T(8,128)(2,1)S(1)}, bf16[1,512,128]{2,1,0:T(8,128)(2,1)}, u32[]{:S(2)}) copy-start(bf16[1,512,128]{2,1,0:T(8,128)(2,1)} %param.6) | copy-start | bytes 393220
  0.0 1.1 %copy-start.2 = (bf16[1,512,128]{2,1,0:T(8,128)(2,1)S(1)}, bf16[1,512,128]{2,1,0:T(8,128)(2,1)}, u32[]{:S(2)}) copy-start(bf16[1,512,128]{2,1,0:T(8,128)(2,1)} %param.7) | copy-start | bytes 393220
  1.8 11.4 %collective-permute-start = (bf16[1024,128]{1,0:T(8,128)(2,1)S(1)}, bf16[1024,128]{1,0:T(8,128)(2,1)S(1)}, u32[]{:S(2)}, u32[]{:S(2)}) collective-permute-start(bf16[1024,128]{1,0:T(8,128)(2,1)S(1)} %get-tuple-element.18), channel_id=1, source_target_pairs={{0,4},{4,8},{8,12},{12,0},{1,5},{5,9},{9,13},{13,1},{2,6},{6,10},{... | collective-permute-start | bytes 786440 | tf_op jit(solution)/shard_map/ppermute | solution.py:123
  13.2 4.3 %copy-start.3 = (bf16[1024,128]{1,0:T(8,128)(2,1)}, bf16[1024,128]{1,0:T(8,128)(2,1)S(1)}, u32[]{:S(2)}) copy-start(bf16[1024,128]{1,0:T(8,128)(2,1)S(1)} %collective-permute-done.kv_ref) | copy-start | bytes 786436
  13.2 15.9 %collective-permute-start.1 = (bf16[1024,128]{1,0:T(8,128)(2,1)S(1)}, bf16[1024,128]{1,0:T(8,128)(2,1)S(1)}, u32[]{:S(2)}, u32[]{:S(2)}) collective-permute-start(bf16[1024,128]{1,0:T(8,128)(2,1)S(1)} %collective-permute-done.kv_ref), channel_id=1, source_target_pairs={{0,4},{4,8},{8,12},{12,0},{1,5},{5,9},{9,13},{13,1},{2,6},{6,10},{... | collective-permute-start | bytes 786440 | tf_op jit(solution)/shard_map/ppermute | solution.py:127
  21.6 13.2 %collective-permute-start.2 = (bf16[512,128]{1,0:T(8,128)(2,1)}, bf16[512,128]{1,0:T(8,128)(2,1)S(1)}, u32[]{:S(2)}, u32[]{:S(2)}) collective-permute-start(bf16[512,128]{1,0:T(8,128)(2,1)} %shard_map.58), channel_id=1, source_target_pairs={{0,12},{4,0},{8,4},{12,8},{1,13},{5,1},{9,5},{13,9},{2,14},{6,2},{... | collective-permute-start | bytes 393224 | tf_op jit(solution)/shard_map/ppermute | solution.py:130
  29.2 0.7 %copy-start.4 = (bf16[1024,128]{1,0:T(8,128)(2,1)}, bf16[1024,128]{1,0:T(8,128)(2,1)S(1)}, u32[]{:S(2)}) copy-start(bf16[1024,128]{1,0:T(8,128)(2,1)S(1)} %collective-permute-done.1.kv_ref) | copy-start | bytes 786436
  33.6 1.2 %copy-start.1 = (f32[512,128]{1,0:T(8,128)S(1)}, f32[512,128]{1,0:T(8,128)}, u32[]{:S(2)}) copy-start(f32[512,128]{1,0:T(8,128)} %get-tuple-element.15) | copy-start | bytes 786436
